TPU v7x, 512 devices: a whole 4x8x8 slice. The times are simulated.
512 devices in a mesh: doc: 16 (over z_lo, y), label: 32 (over x, z_hi, core).
Axes of the slice: x: 4, y: 8, z: 8 (z_hi: 4, z_lo: 2; z = z_hi * 2 + z_lo), core: 2. Of those that a mesh axis runs over, the one named last changes fastest.
Arguments:
- doc_embed: bfloat16 [16384, 768], P(('doc', 'label')), may hold values from -0.59765625 to 0.59765625
- classifier: bfloat16 [32768, 768], P('label'), may hold values from -4.28125 to 4.28125
- centroids: bfloat16 [256, 768], P('doc'), may hold values from -4.28125 to 4.28125
- shortlist: int32 [16384, 32], P(('doc', 'label')), may hold values from 0 to 255, all different within a row
- positives: int32 [16384, 4], P(('doc', 'label')), may hold values from 0 to 4095
Outputs:
- grad_classifier: bfloat16 [32768, 768], P('label')
- grad_centroids: float32 [256, 768], P('doc')
- grad_docs: bfloat16 [16384, 768], P(('doc', 'label'))
Inputs may be any that keep to these rules, and one draw needn't show every extreme that they name: `shortlist`: each row names 32 different clusters; every cluster is named by some row.
All inputs are finite; a program needn't handle non-finite values.
Results may differ from a plain program's by a relative error of at most 0.015.
Values may be sent and summed in bfloat16 or wider, within the bound.
No kernel may reach another device: no remote copies, remote signals or barrier semaphores. Data moves between devices by JAX's collectives and lax.ppermute only.
A program may use at most 64 MiB of HBM per device.

v0:
```python
import jax
import jax.numpy as jnp
from jax import lax
from jax.sharding import PartitionSpec as P

CLS = 128


LOSS_WEIGHT = 0.125


def tile_grads(rows, short_rows, pos_rows, classifier, cent_rows, cluster_base):
    labels_dev = classifier.shape[0]
    local_clusters = cluster_base + jnp.arange(labels_dev // CLS, dtype=jnp.int32)
    local_labels = cluster_base * CLS + jnp.arange(labels_dev, dtype=jnp.int32)
    logits = jnp.einsum("nd,ld->nl", rows, classifier, preferred_element_type=jnp.float32)
    member = jnp.any(short_rows[:, :, None] == local_clusters[None, None, :], axis=1)
    mask = jnp.repeat(member, CLS, axis=1)
    target = jnp.any(pos_rows[:, :, None] == local_labels[None, None, :], axis=1)
    grad = (
        LOSS_WEIGHT
        * (jax.nn.sigmoid(logits) - target.astype(jnp.float32))
        * mask.astype(jnp.float32)
    ).astype(jnp.bfloat16)
    meta_logits = jnp.einsum("nd,cd->nc", rows, cent_rows, preferred_element_type=jnp.float32)
    pos_clusters = pos_rows // CLS
    meta_target = jnp.any(pos_clusters[:, :, None] == local_clusters[None, None, :], axis=1)
    meta_grad = (
        LOSS_WEIGHT * (jax.nn.sigmoid(meta_logits) - meta_target.astype(jnp.float32))
    ).astype(jnp.bfloat16)
    return (grad, meta_grad)


def body(doc_embed, classifier, centroids, shortlist, positives):
    labels_dev = classifier.shape[0]
    cl_here = labels_dev // CLS
    per_doc = centroids.shape[0]
    label_index = lax.axis_index("label")
    cluster_base = label_index * cl_here
    pos_cluster = jnp.take_along_axis(shortlist, positives // CLS, axis=1)
    pos_label = pos_cluster * CLS + positives % CLS
    all_cent = lax.all_gather(centroids, "doc", axis=0, tiled=True)
    cent_rows = lax.dynamic_slice_in_dim(all_cent, cluster_base, cl_here, 0)
    rows, short_rows, pos_rows = (
        lax.all_gather(doc_embed, "label", axis=0, tiled=True),
        lax.all_gather(shortlist, "label", axis=0, tiled=True),
        lax.all_gather(pos_label, "label", axis=0, tiled=True),
    )
    grad, meta_grad = tile_grads(rows, short_rows, pos_rows, classifier, cent_rows, cluster_base)
    class_acc = jnp.einsum("nl,nd->ld", grad, rows, preferred_element_type=jnp.float32)
    cent_acc = jnp.einsum("nc,nd->cd", meta_grad, rows, preferred_element_type=jnp.float32)
    input_sum = lax.psum_scatter(
        (
            jnp.dot(grad, classifier, preferred_element_type=jnp.float32)
            + jnp.dot(meta_grad, cent_rows, preferred_element_type=jnp.float32)
        ).astype(jnp.bfloat16),
        "label",
        scatter_dimension=0,
        tiled=True,
    )
    grad_classifier = lax.psum(class_acc.astype(jnp.bfloat16), "doc")
    cent_summed = lax.psum(cent_acc, "doc")
    cent_whole = lax.all_gather(cent_summed, "label", axis=0, tiled=True)
    grad_centroids = lax.dynamic_slice_in_dim(
        cent_whole, lax.axis_index("doc") * per_doc, per_doc, 0
    )
    return (grad_classifier, grad_centroids, input_sum)


def solution(mesh):
    in_specs = (
        P(("doc", "label"), None),
        P("label", None),
        P("doc", None),
        P(("doc", "label"), None),
        P(("doc", "label"), None),
    )
    out_specs = (P("label", None), P("doc", None), P(("doc", "label"), None))
    return jax.shard_map(body, mesh=mesh, in_specs=in_specs, out_specs=out_specs, check_vma=False)
```

profile of v0, /device:TPU:8, one launch (start us, length us, event | category | flops | bytes accessed | tf_op | source)
XLA Modules:
  0.0 373.3 jit_solution(2617783042345759563)
XLA Ops:
  7.2 0.7 all-gather.3.cloned.1.call-update
  8.0 0.7 bitcast_or_fusion
  8.8 0.1 reshape.31
  8.9 1.3 gather_fusion
  10.4 50.2 %all-gather = s32[32,32,4]{1,2,0:T(4,128)S(1)} all-gather(s32[1,32,4]{1,2,0:T(4,128)S(1)} %fusion.12), channel_id=1, replica_groups=mesh['doc'=16,'label'=32] {'label'}, dimensions={0}, use_global_device_ids=true | all-gather | bytes 16896 | tf_op jit(solution)/shard_map/all_gather | solution.py:47
  60.7 41.3 %all_gather.15 = s32[1024,32]{1,0:T(8,128)S(1)} all-gather(s32[32,32]{1,0:T(8,128)S(1)} %copy-done.1), channel_id=1, replica_groups=mesh['doc'=16,'label'=32] {'label'}, dimensions={0}, use_global_device_ids=true | all-gather | bytes 135168 | tf_op jit(solution)/shard_map/all_gather | solution.py:46
  102.1 0.2 copy.45
  102.2 0.2 compare_reduce_fusion.1
  102.5 0.3 copy.46
  102.7 3.8 %compare_reduce_fusion = pred[1024,1024]{1,0:T(8,128)(4,1)} fusion(s32[1024]{0:T(1024)S(1)} %iota_add_fusion, s32[1024,4]{0,1:T(4,128)S(1)} %reshape.43), kind=kLoop, calls=%fused_computation.1 | loop fusion | flops 7340032 | bytes 1069056 | tf_op jit(solution)/shard_map/reduce_or | solution.py:19
  106.6 3.2 broadcast_in_dim.6
  109.7 4.6 %select_convert_fusion = bf16[1024,1024]{1,0:T(8,128)(2,1)S(1)} fusion(pred[1024,1024]{1,0:T(8,128)(4,1)} %compare_reduce_fusion, pred[128,8,8,128]{3,2,1,0:T(8,128)(4,1)S(1)} %bitcast.29, bf16[1024,768]{1,0:T(8,128)(2,1)} %all-gather.3.cloned.1.call-done, bf16[1024,768]{1,0:T(8,128)(2,1)S(1)} %copy-done), kind=kOutput, calls=%fused_computation.2 | convolution fusion | flops 1619001344 | bytes 7340032 | tf_op jit(solution)/shard_map/nd,ld->nl/dot_general | solution.py:16
  114.3 1.3 copy-done.5
  115.7 3.0 convolution_convert_fusion
  118.9 35.4 %all_gather.18 = bf16[256,768]{1,0:T(8,128)(2,1)S(1)} all-gather(bf16[16,768]{1,0:T(8,128)(2,1)S(1)} %copy-done.3), channel_id=1, replica_groups=mesh['doc'=16,'label'=32] {'doc'}, dimensions={0}, use_global_device_ids=true | all-gather | bytes 417792 | tf_op jit(solution)/shard_map/all_gather | solution.py:42
  154.3 0.5 fusion.6
  154.8 3.4 fusion.17
  158.2 1.8 add_convert_fusion
  160.1 0.3 fusion.16
  160.4 59.2 %psum.15 = f32[8,768]{1,0:T(8,128)S(1)} all-reduce(f32[8,768]{1,0:T(8,128)S(1)} %fusion.16), channel_id=1, replica_groups=mesh['doc'=16,'label'=32] {'doc'}, use_global_device_ids=true, to_apply=%region_4.5 | all-reduce | flops 6144 | bytes 49152 | tf_op jit(solution)/shard_map/psum | solution.py:62
  219.6 44.9 %all_gather.19 = f32[256,768]{1,0:T(8,128)S(1)} all-gather(f32[8,768]{1,0:T(8,128)S(1)} %psum.15), channel_id=1, replica_groups=mesh['doc'=16,'label'=32] {'label'}, dimensions={0}, use_global_device_ids=true | all-gather | bytes 811008 | tf_op jit(solution)/shard_map/all_gather | solution.py:63
  264.5 0.6 constant_dynamic-slice_fusion
  265.1 99.0 %reduce-scatter.2.cloned.1.call-done = bf16[32,768]{1,0:T(8,128)(2,1)} async-done(((bf16[1024,768]{1,0:T(8,128)(2,1)}), bf16[32,768]{1,0:T(8,128)(2,1)}) %reduce-scatter.2.cloned.1.call-update) | async-done | bytes 49168 | tf_op jit(solution)/shard_map/reduce_scatter | solution.py:52
  364.1 2.7 copy.53
  (28 shorter events, 0.7 us)
Async XLA Ops:
  7.2 102.6 %copy-start = (bf16[1024,768]{1,0:T(8,128)(2,1)S(1)}, bf16[1024,768]{1,0:T(8,128)(2,1)}, u32[]{:S(2)}) copy-start(bf16[1024,768]{1,0:T(8,128)(2,1)} %param.6) | copy-start | bytes 4718596
  7.2 1.7 copy-start.1
  7.2 99.4 %all-gather.3.cloned.1.call-start = ((), (), s32[]{:S(2)}) async-start(), calls=%async_computation.1 | async-start | bytes 1622016 | tf_op jit(solution)/shard_map/all_gather | solution.py:45
  7.9 257.2 %all-reduce.2.cloned.1.call-start = ((), (), s32[]{:S(2)}) async-start(), calls=%async_computation.2 | async-start | bytes 3145728 | tf_op jit(solution)/shard_map/psum | solution.py:61
  8.9 1.5 copy-start.4
  109.7 5.9 %copy-start.2 = (bf16[1024,768]{1,0:T(8,128)(2,1)S(1)}, bf16[1024,768]{1,0:T(8,128)(2,1)}, u32[]{:S(2)}) copy-start(bf16[1024,768]{1,0:T(8,128)(2,1)} %all-gather.3.cloned.1.call-done) | copy-start | bytes 4718596
  114.3 1.4 copy-start.5
  115.7 3.2 copy-start.3
  118.7 245.4 %reduce-scatter.2.cloned.1.call-start = ((), (), s32[]{:S(2)}) async-start(), calls=%async_computation.3 | async-start | bytes 1622016 | tf_op jit(solution)/shard_map/reduce_scatter | solution.py:52
Sparse Core Ops, SparseCore 0:
  11.1 64.0 all-gather.2
  118.9 141.9 all-reduce.1
  265.9 98.2 reduce-scatter.1
where the time goes:
time: 374 us; the launch traced here: 373 us
  blocking collectives  231 us (62%)
  waiting for transfers between devices  99.7 us (27%)
  between operations  13.9 us (4%)
  matrix products  13.6 us (4%)
  local copies, waits for them, and re-layouts  9.97 us (3%)
  other arithmetic  4.87 us (1%)
    reduce_scatter x1, waiting for transfers between devices, body(): lax.psum_scatter((jnp.dot(grad, classifier, preferred_element_type=jnp.fl...  99 us
    psum x1, blocking collectives, body(): cent_summed = lax.psum(cent_acc, 'doc')  59.2 us
    all_gather x1, blocking collectives, body(): lax.all_gather(pos_label, 'label', axis=0, tiled=True)  50.2 us
    all_gather x1, blocking collectives, body(): cent_whole = lax.all_gather(cent_summed, 'label', axis=0, tiled=True)  44.9 us
    all_gather x1, blocking collectives, body(): lax.all_gather(shortlist, 'label', axis=0, tiled=True)  41.3 us
    all_gather x1, blocking collectives, body(): all_cent = lax.all_gather(centroids, 'doc', axis=0, tiled=True)  35.4 us
  transfers between devices with their start and end apart: 3, of which 1 were waited for; matrix products, arithmetic and copies ran while one was open for 4% of the time, Pallas kernels for 0%

commit v1 on v0

v1 whole, which is shorter than its diff:
```python
import jax
import jax.numpy as jnp
from jax import lax
from jax.sharding import PartitionSpec as P


CLS = 128
LOSS_WEIGHT = 0.125


def step(doc_embed, classifier, centroids, shortlist, positives):
    n_doc = lax.axis_size("doc")
    labels_dev, width = classifier.shape
    cl_here = labels_dev // CLS
    per_doc = centroids.shape[0]
    docs_dev, short = shortlist.shape
    n_pos = positives.shape[1]
    label_index = lax.axis_index("label")
    cluster_base = label_index * cl_here

    pos_cluster = jnp.take_along_axis(shortlist, positives // CLS, axis=1)
    ints = jnp.concatenate([shortlist, pos_cluster, positives % CLS], axis=1).astype(jnp.bfloat16)
    pad = (-(width + ints.shape[1])) % 128
    packed = jnp.concatenate(
        [doc_embed, ints, jnp.zeros((docs_dev, pad), jnp.bfloat16)], axis=1
    )
    gathered = lax.all_gather(packed, "label", axis=0, tiled=True)
    all_cent = lax.all_gather(centroids, "doc", axis=0, tiled=True)
    gathered, all_cent = lax.optimization_barrier((gathered, all_cent))
    rows = gathered[:, :width]
    ints_rows = gathered[:, width : width + short + 2 * n_pos].astype(jnp.int32)
    short_rows = ints_rows[:, :short]
    pcl_rows = ints_rows[:, short : short + n_pos]
    pos_rows = pcl_rows * CLS + ints_rows[:, short + n_pos :]

    n_clusters = all_cent.shape[0]

    local_clusters = cluster_base + jnp.arange(cl_here, dtype=jnp.int32)
    local_labels = cluster_base * CLS + jnp.arange(labels_dev, dtype=jnp.int32)
    logits = jnp.einsum("nd,ld->nl", rows, classifier, preferred_element_type=jnp.float32)
    member = jnp.any(short_rows[:, :, None] == local_clusters[None, None, :], axis=1)
    mask = jnp.repeat(member, CLS, axis=1)
    target = jnp.any(pos_rows[:, :, None] == local_labels[None, None, :], axis=1)
    grad = (
        LOSS_WEIGHT
        * (jax.nn.sigmoid(logits) - target.astype(jnp.float32))
        * mask.astype(jnp.float32)
    ).astype(jnp.bfloat16)

    docs_part = jnp.dot(grad, classifier, preferred_element_type=jnp.float32).astype(jnp.bfloat16)
    docs_sum = lax.psum_scatter(docs_part, "label", scatter_dimension=0, tiled=True)

    meta_logits = jnp.einsum("nd,cd->nc", rows, all_cent, preferred_element_type=jnp.float32)
    cluster_ids = jnp.arange(n_clusters, dtype=jnp.int32)
    meta_target = jnp.any(pcl_rows[:, :, None] == cluster_ids[None, None, :], axis=1)
    meta_grad = (
        LOSS_WEIGHT * (jax.nn.sigmoid(meta_logits) - meta_target.astype(jnp.float32))
    ).astype(jnp.bfloat16)
    cent_part = jnp.einsum("nc,nd->cd", meta_grad, rows, preferred_element_type=jnp.float32)
    cent_hi = cent_part.astype(jnp.bfloat16)
    cent_lo = (cent_part - cent_hi.astype(jnp.float32)).astype(jnp.bfloat16)

    class_part = jnp.einsum("nl,nd->ld", grad, rows, preferred_element_type=jnp.float32).astype(jnp.bfloat16)
    sub = labels_dev // n_doc
    send = jnp.concatenate(
        [
            class_part.reshape(n_doc, sub, width),
            cent_hi.reshape(n_doc, per_doc, width),
            cent_lo.reshape(n_doc, per_doc, width),
        ],
        axis=1,
    ).reshape(n_doc * (sub + 2 * per_doc), width)
    recv = lax.all_to_all(send, "doc", 0, 0, tiled=True)
    recv = recv.reshape(n_doc, sub + 2 * per_doc, width)
    class_sum = jnp.sum(recv[:, :sub].astype(jnp.float32), axis=0).astype(jnp.bfloat16)
    grad_centroids = jnp.sum(
        recv[:, sub : sub + per_doc].astype(jnp.float32)
        + recv[:, sub + per_doc :].astype(jnp.float32),
        axis=0,
    )
    spread = jnp.broadcast_to(class_sum[None], (n_doc, sub, width)).reshape(n_doc * sub, width)
    grad_classifier = lax.all_to_all(spread, "doc", 0, 0, tiled=True)

    local_meta = lax.dynamic_slice_in_dim(meta_grad, label_index * docs_dev, docs_dev, 0)
    meta_term = jnp.dot(local_meta, all_cent, preferred_element_type=jnp.float32)
    grad_docs = (docs_sum.astype(jnp.float32) + meta_term).astype(jnp.bfloat16)
    return (grad_classifier, grad_centroids, grad_docs)


def solution(mesh):
    in_specs = (
        P(("doc", "label"), None),
        P("label", None),
        P("doc", None),
        P(("doc", "label"), None),
        P(("doc", "label"), None),
    )
    out_specs = (P("label", None), P("doc", None), P(("doc", "label"), None))
    return jax.shard_map(step, mesh=mesh, in_specs=in_specs, out_specs=out_specs, check_vma=False)
```

time: 374 us -> 279 us (0.75)
  blocking collectives: 231 us -> 103 us
  waiting for transfers between devices: 99.7 us -> 122 us
  starting transfers between devices: 0.12 us -> 4.35 us
    all_gather x4 -> x1, blocking collectives: 172 us -> 40.1 us  [step(): all_cent = lax.all_gather(centroids, 'doc', axis=0, tiled=True)]
    all_to_all x0 -> x1, blocking collectives: none -> 62.8 us  [step(): recv = lax.all_to_all(send, 'doc', 0, 0, tiled=True)]
    psum x1 -> x0, blocking collectives: 59.2 us -> none  [body(): cent_summed = lax.psum(cent_acc, 'doc')]
    all_gather x1, waiting for transfers between devices: 0.01 us -> 24.1 us  [step(): gathered = lax.all_gather(packed, 'label', axis=0, tiled=True)]
    all_to_all x0 -> x1, starting transfers between devices: none -> 4.27 us  [step(): grad_classifier = lax.all_to_all(spread, 'doc', 0, 0, tiled=True)]
  transfers between devices with their start and end apart: 3 -> 3, of which waited for: 1 -> 2; matrix products, arithmetic and copies ran while one was open for 4% -> 3% of each run, Pallas kernels for 0% -> 0%
where the time goes in v1:
time: 279 us; the launch traced here: 278 us
  waiting for transfers between devices  122 us (44%)
  blocking collectives  103 us (37%)
  between operations  14.3 us (5%)
  matrix products  13.7 us (5%)
  local copies, waits for them, and re-layouts  12.8 us (5%)
  other arithmetic  8.59 us (3%)
  starting transfers between devices  4.35 us (2%)
    reduce_scatter x1, waiting for transfers between devices, step(): lax.psum_scatter(docs_part, 'label', scatter_dimension=0, tiled=True)  97.6 us
    all_to_all x1, blocking collectives, step(): recv = lax.all_to_all(send, 'doc', 0, 0, tiled=True)  62.8 us
    all_gather x1, blocking collectives, step(): all_cent = lax.all_gather(centroids, 'doc', axis=0, tiled=True)  40.1 us
    all_gather x1, waiting for transfers between devices, step(): gathered = lax.all_gather(packed, 'label', axis=0, tiled=True)  24.1 us
  transfers between devices with their start and end apart: 3, of which 2 were waited for; matrix products, arithmetic and copies ran while one was open for 3% of the time, Pallas kernels for 0%

profile of v1, /device:TPU:8, one launch (start us, length us, event | category | flops | bytes accessed | tf_op | source)
XLA Modules:
  0.0 278.4 jit_solution(8035683662085940447)
XLA Ops:
  7.2 0.8 fusion.14
  8.0 0.7 bitcast_or_fusion
  8.8 0.7 convert.10
  9.8 1.3 gather_fusion
  11.4 0.7 concatenate.9
  12.2 40.1 %all_gather.7 = bf16[256,768]{1,0:T(8,128)(2,1)} all-gather(bf16[16,768]{1,0:T(8,128)(2,1)S(1)} %copy-done.6), channel_id=1, replica_groups=mesh['doc'=16,'label'=32] {'doc'}, dimensions={0}, use_global_device_ids=true | all-gather | bytes 417792 | tf_op jit(solution)/shard_map/all_gather | solution.py:28
  52.3 24.1 %all-gather.2.cloned.1.call-done = bf16[1024,896]{1,0:T(8,128)(2,1)} async-done(((bf16[32,896]{1,0:T(8,128)(2,1)}), bf16[1024,896]{1,0:T(8,128)(2,1)}) %all-gather.2.cloned.1.call-update) | async-done | bytes 1835024 | tf_op jit(solution)/shard_map/all_gather | solution.py:27
  76.4 2.9 %copy.39 = bf16[1024,896]{0,1:T(8,128)(2,1)S(1)} copy(bf16[1024,896]{1,0:T(8,128)(2,1)} %all-gather.2.cloned.1.call-done) | data formatting | bytes 3670016 | tf_op jit(solution)/shard_map/optimization_barrier | solution.py:29
  79.8 1.0 fusion
  80.8 2.3 fusion.6
  83.1 0.6 subtract_convert_fusion
  83.7 2.8 %compare_reduce_fusion = pred[1024,1024]{1,0:T(8,128)(4,1)S(1)} fusion(s32[1024]{0:T(1024)S(1)} %iota_add_fusion, s32[1024,4]{0,1:T(4,128)S(1)} %get-tuple-element.11), kind=kLoop, calls=%fused_computation.1 | loop fusion | flops 7340032 | bytes 1069056 | tf_op jit(solution)/shard_map/reduce_or | solution.py:43
  86.6 3.2 %broadcast_in_dim.12 = pred[1024,8,128]{2,1,0:T(8,128)(4,1)S(1)} broadcast(pred[1024,8]{1,0:T(8,128)(4,1)S(1)} %copy.40), dimensions={0,1} | broadcast | bytes 1056768 | tf_op jit(solution)/shard_map/broadcast_in_dim | solution.py:42
  89.8 2.7 select_convert_fusion
  92.5 1.9 convolution_convert_fusion.1
  94.6 62.8 %all_to_all.15 = bf16[16,96,768]{2,1,0:T(8,128)(2,1)S(1)} all-to-all(bf16[16,96,768]{2,1,0:T(8,128)(2,1)S(1)} %pad_maximum_fusion), channel_id=1, replica_groups=mesh['doc'=16,'label'=32] {'doc'}, dimensions={0} | all-to-all | bytes 4718592 | tf_op jit(solution)/shard_map/all_to_all | solution.py:73
  157.4 1.4 copy-done.2
  159.0 1.3 broadcast_in_dim.13
  160.3 4.3 %all-to-all-start.1 = ((bf16[16,64,768]{2,1,0:T(8,128)(2,1)}), bf16[16,64,768]{2,1,0:T(8,128)(2,1)S(1)}, u32[]{:S(2)}, u32[]{:S(2)}) async-start(bf16[16,64,768]{2,1,0:T(8,128)(2,1)} %broadcast_in_dim.13), calls=%async_computation.1 | async-start | bytes 3145728 | tf_op jit(solution)/shard_map/all_to_all | solution.py:82
  164.7 4.6 %convolution_convert_fusion = bf16[1024,768]{1,0:T(8,128)(2,1)} fusion(bf16[1024,1024]{1,0:T(8,128)(2,1)} %copy-done.8, bf16[1024,768]{1,0:T(8,128)(2,1)S(1)} %copy-done), kind=kOutput, calls=%fused_computation.6 | convolution fusion | flops 1611399168 | bytes 5242880 | tf_op jit(solution)/shard_map/dot_general | solution.py:50
  169.3 97.6 %reduce-scatter.2.cloned.1.call-done = bf16[32,768]{1,0:T(8,128)(2,1)} async-done(((bf16[1024,768]{1,0:T(8,128)(2,1)}), bf16[32,768]{1,0:T(8,128)(2,1)}) %reduce-scatter.2.cloned.1.call-update) | async-done | bytes 49168 | tf_op jit(solution)/shard_map/reduce_scatter | solution.py:51
  266.9 1.6 fusion.7
  268.5 1.8 add_reduce_fusion
  270.4 1.1 copy.44
  (39 shorter events, 1.7 us)
Async XLA Ops:
  7.2 82.6 %copy-start = (bf16[1024,768]{1,0:T(8,128)(2,1)S(1)}, bf16[1024,768]{1,0:T(8,128)(2,1)}, u32[]{:S(2)}) copy-start(bf16[1024,768]{1,0:T(8,128)(2,1)} %param.6) | copy-start | bytes 4718596
  7.2 2.6 copy-start.1
  7.2 69.2 %all-gather.2.cloned.1.call-start = ((), (), s32[]{:S(2)}) async-start(), calls=%async_computation.3 | async-start | bytes 1892352 | tf_op jit(solution)/shard_map/all_gather | solution.py:27
  9.8 1.6 copy-start.5
  9.8 2.4 copy-start.6
  80.8 2.3 copy-start.3
  83.1 3.5 %copy-start.7 = (bf16[1024,256]{1,0:T(8,128)(2,1)}, bf16[1024,256]{1,0:T(8,128)(2,1)S(1)}, u32[]{:S(2)}) copy-start(bf16[1024,256]{1,0:T(8,128)(2,1)S(1)} %fusion.6) | copy-start | bytes 1572868
  92.5 1.9 copy-start.8
  157.4 1.4 copy-start.2
  160.3 110.0 %all-to-all-start.1 = ((bf16[16,64,768]{2,1,0:T(8,128)(2,1)}), bf16[16,64,768]{2,1,0:T(8,128)(2,1)S(1)}, u32[]{:S(2)}, u32[]{:S(2)}) async-start(bf16[16,64,768]{2,1,0:T(8,128)(2,1)} %broadcast_in_dim.13), calls=%async_computation.1 | async-start | bytes 3145728 | tf_op jit(solution)/shard_map/all_to_all | solution.py:82
  164.6 102.3 %copy-start.4 = (bf16[256,768]{1,0:T(8,128)(2,1)S(1)}, bf16[256,768]{1,0:T(8,128)(2,1)}, u32[]{:S(2)}) copy-start(bf16[256,768]{1,0:T(8,128)(2,1)} %all_gather.7) | copy-start | bytes 1179652
  164.6 102.3 %reduce-scatter.2.cloned.1.call-start = ((), (), s32[]{:S(2)}) async-start(), calls=%async_computation.4 | async-start | bytes 1622016 | tf_op jit(solution)/shard_map/reduce_scatter | solution.py:51
Sparse Core Ops, SparseCore 0:
  12.2 64.0 all-gather.1
  169.9 96.9 reduce-scatter.1

commit v2 on v1

--- a/solution.py
+++ b/solution.py
@@ -36,29 +36,32 @@
     n_clusters = all_cent.shape[0]
 
     local_clusters = cluster_base + jnp.arange(cl_here, dtype=jnp.int32)
-    local_labels = cluster_base * CLS + jnp.arange(labels_dev, dtype=jnp.int32)
     logits = jnp.einsum("nd,ld->nl", rows, classifier, preferred_element_type=jnp.float32)
     member = jnp.any(short_rows[:, :, None] == local_clusters[None, None, :], axis=1)
-    mask = jnp.repeat(member, CLS, axis=1)
-    target = jnp.any(pos_rows[:, :, None] == local_labels[None, None, :], axis=1)
+    pos_local = pos_rows - cluster_base * CLS
+    label_ids = jnp.arange(labels_dev, dtype=jnp.int32).reshape(1, cl_here, CLS)
+    target = pos_local[:, 0, None, None] == label_ids
+    for p in range(1, n_pos):
+        target = target | (pos_local[:, p, None, None] == label_ids)
     grad = (
         LOSS_WEIGHT
-        * (jax.nn.sigmoid(logits) - target.astype(jnp.float32))
-        * mask.astype(jnp.float32)
-    ).astype(jnp.bfloat16)
+        * (jax.nn.sigmoid(logits.reshape(-1, cl_here, CLS)) - target.astype(jnp.float32))
+        * member[:, :, None].astype(jnp.float32)
+    ).astype(jnp.bfloat16).reshape(-1, labels_dev)
 
     docs_part = jnp.dot(grad, classifier, preferred_element_type=jnp.float32).astype(jnp.bfloat16)
     docs_sum = lax.psum_scatter(docs_part, "label", scatter_dimension=0, tiled=True)
 
     meta_logits = jnp.einsum("nd,cd->nc", rows, all_cent, preferred_element_type=jnp.float32)
     cluster_ids = jnp.arange(n_clusters, dtype=jnp.int32)
-    meta_target = jnp.any(pcl_rows[:, :, None] == cluster_ids[None, None, :], axis=1)
+    meta_target = pcl_rows[:, 0, None] == cluster_ids[None, :]
+    for p in range(1, n_pos):
+        meta_target = meta_target | (pcl_rows[:, p, None] == cluster_ids[None, :])
     meta_grad = (
         LOSS_WEIGHT * (jax.nn.sigmoid(meta_logits) - meta_target.astype(jnp.float32))
     ).astype(jnp.bfloat16)
     cent_part = jnp.einsum("nc,nd->cd", meta_grad, rows, preferred_element_type=jnp.float32)
     cent_hi = cent_part.astype(jnp.bfloat16)
-    cent_lo = (cent_part - cent_hi.astype(jnp.float32)).astype(jnp.bfloat16)
 
     class_part = jnp.einsum("nl,nd->ld", grad, rows, preferred_element_type=jnp.float32).astype(jnp.bfloat16)
     sub = labels_dev // n_doc
@@ -66,18 +69,13 @@
         [
             class_part.reshape(n_doc, sub, width),
             cent_hi.reshape(n_doc, per_doc, width),
-            cent_lo.reshape(n_doc, per_doc, width),
         ],
         axis=1,
-    ).reshape(n_doc * (sub + 2 * per_doc), width)
+    ).reshape(n_doc * (sub + per_doc), width)
     recv = lax.all_to_all(send, "doc", 0, 0, tiled=True)
-    recv = recv.reshape(n_doc, sub + 2 * per_doc, width)
+    recv = recv.reshape(n_doc, sub + per_doc, width)
     class_sum = jnp.sum(recv[:, :sub].astype(jnp.float32), axis=0).astype(jnp.bfloat16)
-    grad_centroids = jnp.sum(
-        recv[:, sub : sub + per_doc].astype(jnp.float32)
-        + recv[:, sub + per_doc :].astype(jnp.float32),
-        axis=0,
-    )
+    grad_centroids = jnp.sum(recv[:, sub:].astype(jnp.float32), axis=0)
     spread = jnp.broadcast_to(class_sum[None], (n_doc, sub, width)).reshape(n_doc * sub, width)
     grad_classifier = lax.all_to_all(spread, "doc", 0, 0, tiled=True)
 

time: 279 us -> 265 us (0.950)
  blocking collectives: 103 us -> 91.4 us
  other arithmetic: 8.59 us -> 4.83 us
    all_to_all x1, blocking collectives: 62.8 us -> 53.9 us  [step(): recv = lax.all_to_all(send, 'doc', 0, 0, tiled=True)]
    reduce_or x2 -> x0, other arithmetic: 3.84 us -> none  [the longest x1 2.83 us: step(): jnp.any(pos_rows[:, :, None] == local_labels[None, None, :], axis=1)]
    broadcast_in_dim x1 -> x0, local copies, waits for them, and re-layouts: 3.18 us -> none  [step(): mask = jnp.repeat(member, CLS, axis=1)]
    optimization_barrier x1 -> x0, local copies, waits for them, and re-layouts: 2.89 us -> none  [step(): gathered, all_cent = lax.optimization_barrier((gathered, all_cent))]
where the time goes in v2:
time: 265 us
  waiting for transfers between devices  124 us (47%)
  blocking collectives  91.4 us (34%)
  between operations  14.3 us (5%)
  matrix products  14.1 us (5%)
  local copies, waits for them, and re-layouts  10.8 us (4%)
  starting transfers between devices  4.83 us (2%)
  other arithmetic  4.83 us (2%)
    reduce_scatter x1, waiting for transfers between devices, step(): lax.psum_scatter(docs_part, 'label', scatter_dimension=0, tiled=True)  97.7 us
    all_to_all x1, blocking collectives, step(): recv = lax.all_to_all(send, 'doc', 0, 0, tiled=True)  53.9 us
    all_gather x1, blocking collectives, step(): all_cent = lax.all_gather(centroids, 'doc', axis=0, tiled=True)  37.5 us
    all_gather x1, waiting for transfers between devices, step(): gathered = lax.all_gather(packed, 'label', axis=0, tiled=True)  26.7 us
  transfers between devices with their start and end apart: 3, of which 2 were waited for; matrix products, arithmetic and copies ran while one was open for 3% of the time, Pallas kernels for 0%

profile of v2, /device:TPU:8, one launch (start us, length us, event | category | flops | bytes accessed | tf_op | source)
XLA Modules:
  0.0 264.6 jit_solution(8569315289035908275)
XLA Ops:
  7.2 0.8 bitcast_or_fusion
  8.0 0.7 fusion.17
  8.9 0.7 convert.10
  9.7 1.3 gather_fusion
  11.4 0.7 concatenate.9
  12.1 37.5 %all_gather.7 = bf16[256,768]{1,0:T(8,128)(2,1)S(1)} all-gather(bf16[16,768]{1,0:T(8,128)(2,1)S(1)} %copy-done.5), channel_id=1, replica_groups=mesh['doc'=16,'label'=32] {'doc'}, dimensions={0}, use_global_device_ids=true | all-gather | bytes 417792 | tf_op jit(solution)/shard_map/all_gather | solution.py:28
  49.6 26.7 %all-gather.2.cloned.1.call-done = bf16[1024,896]{1,0:T(8,128)(2,1)} async-done(((bf16[32,896]{1,0:T(8,128)(2,1)}), bf16[1024,896]{1,0:T(8,128)(2,1)}) %all-gather.2.cloned.1.call-update) | async-done | bytes 1835024 | tf_op jit(solution)/shard_map/all_gather | solution.py:27
  76.4 1.0 slice_convert_fusion
  77.4 1.2 slice_reduce_fusion.4
  78.9 1.0 slice_reduce_fusion.8
  80.5 1.1 mul.44
  81.7 0.3 copy-done.4
  82.0 3.6 %fusion = bf16[1024,1024]{1,0:T(8,128)(2,1)S(1)} fusion(f32[128,8,8,128]{3,2,1,0:T(8,128)S(1)} %bitcast.23, bf16[1024,768]{1,0:T(8,128)(2,1)S(1)} %copy-done, s32[1024]{0:T(1024)S(1)} %add_bitcast_fusion, s32[1024]{0:T(1024)S(1)} %get-tuple-element.8, s32[1024]{0:T(1024)S(1)} %get-tuple-element.9, s32[1024]{0:T(1024)S(1)} %get-tuple-element.10, ...), kind=kOutput, calls=%fused_computation.2 | convolution fusion | flops 1625292800 | bytes 9457664 | tf_op jit(solution)/shard_map/nd,ld->nl/dot_general | solution.py:39
  85.7 1.9 convolution_convert_fusion.1
  87.6 1.6 fusion.6
  89.2 0.6 convolution_convert_fusion.2
  90.2 53.9 %all_to_all.15 = bf16[16,80,768]{2,1,0:T(8,128)(2,1)S(1)} all-to-all(bf16[16,80,768]{2,1,0:T(8,128)(2,1)S(1)} %pad_maximum_fusion), channel_id=1, replica_groups=mesh['doc'=16,'label'=32] {'doc'}, dimensions={0} | all-to-all | bytes 3932160 | tf_op jit(solution)/shard_map/all_to_all | solution.py:75
  144.2 1.3 broadcast_in_dim.10
  145.5 4.8 %all-to-all-start.1 = ((bf16[16,64,768]{2,1,0:T(8,128)(2,1)}), bf16[16,64,768]{2,1,0:T(8,128)(2,1)}, u32[]{:S(2)}, u32[]{:S(2)}) async-start(bf16[16,64,768]{2,1,0:T(8,128)(2,1)} %broadcast_in_dim.10), calls=%async_computation.1 | async-start | bytes 3145728 | tf_op jit(solution)/shard_map/all_to_all | solution.py:80
  150.3 4.6 %convolution_convert_fusion = bf16[1024,768]{1,0:T(8,128)(2,1)} fusion(bf16[1024,1024]{1,0:T(8,128)(2,1)} %copy-done.7, bf16[1024,768]{1,0:T(8,128)(2,1)S(1)} %copy-done), kind=kOutput, calls=%fused_computation.4 | convolution fusion | flops 1611399168 | bytes 5242880 | tf_op jit(solution)/shard_map/dot_general | solution.py:52
  154.9 97.7 %reduce-scatter.2.cloned.1.call-done = bf16[32,768]{1,0:T(8,128)(2,1)} async-done(((bf16[1024,768]{1,0:T(8,128)(2,1)}), bf16[32,768]{1,0:T(8,128)(2,1)}) %reduce-scatter.2.cloned.1.call-update) | async-done | bytes 49168 | tf_op jit(solution)/shard_map/reduce_scatter | solution.py:53
  252.6 1.8 fusion.7
  254.5 0.7 convert_reduce_fusion
  255.1 2.7 %copy.37 = bf16[1024,768]{1,0:T(8,128)(2,1)} copy(bf16[1024,768]{1,0:T(8,128)(2,1)} %bitcast.4) | data formatting | bytes 3145728
  (37 shorter events, 2.2 us)
Async XLA Ops:
  7.2 74.5 %copy-start = (bf16[1024,768]{1,0:T(8,128)(2,1)S(1)}, bf16[1024,768]{1,0:T(8,128)(2,1)}, u32[]{:S(2)}) copy-start(bf16[1024,768]{1,0:T(8,128)(2,1)} %param.6) | copy-start | bytes 4718596
  7.2 2.5 copy-start.1
  7.2 69.2 %all-gather.2.cloned.1.call-start = ((), (), s32[]{:S(2)}) async-start(), calls=%async_computation.3 | async-start | bytes 1892352 | tf_op jit(solution)/shard_map/all_gather | solution.py:27
  9.7 1.7 copy-start.3
  9.7 2.5 copy-start.5
  49.6 37.9 %copy-start.2 = (bf16[256,768]{1,0:T(8,128)(2,1)}, bf16[256,768]{1,0:T(8,128)(2,1)S(1)}, u32[]{:S(2)}) copy-start(bf16[256,768]{1,0:T(8,128)(2,1)S(1)} %all_gather.7) | copy-start | bytes 1179652
  80.5 1.5 copy-start.4
  85.7 1.9 copy-start.7
  89.2 0.8 copy-start.6
  145.5 109.6 %all-to-all-start.1 = ((bf16[16,64,768]{2,1,0:T(8,128)(2,1)}), bf16[16,64,768]{2,1,0:T(8,128)(2,1)}, u32[]{:S(2)}, u32[]{:S(2)}) async-start(bf16[16,64,768]{2,1,0:T(8,128)(2,1)} %broadcast_in_dim.10), calls=%async_computation.1 | async-start | bytes 3145728 | tf_op jit(solution)/shard_map/all_to_all | solution.py:80
  150.3 102.4 %reduce-scatter.2.cloned.1.call-start = ((), (), s32[]{:S(2)}) async-start(), calls=%async_computation.4 | async-start | bytes 1622016 | tf_op jit(solution)/shard_map/reduce_scatter | solution.py:53
Sparse Core Ops, SparseCore 0:
  12.2 64.0 all-gather.1
  155.5 97.0 reduce-scatter.1

commit v3 on v2

--- a/solution.py
+++ b/solution.py
@@ -18,27 +18,31 @@
     label_index = lax.axis_index("label")
     cluster_base = label_index * cl_here
 
+    n_label = lax.axis_size("label")
     pos_cluster = jnp.take_along_axis(shortlist, positives // CLS, axis=1)
-    ints = jnp.concatenate([shortlist, pos_cluster, positives % CLS], axis=1).astype(jnp.bfloat16)
-    pad = (-(width + ints.shape[1])) % 128
-    packed = jnp.concatenate(
-        [doc_embed, ints, jnp.zeros((docs_dev, pad), jnp.bfloat16)], axis=1
+    ints = jnp.concatenate([shortlist, pos_cluster, positives % CLS], axis=1)
+    ints_rows = lax.all_to_all(
+        jnp.broadcast_to(ints[None], (n_label,) + ints.shape).reshape(n_label * docs_dev, -1),
+        "label", 0, 0, tiled=True,
     )
-    gathered = lax.all_gather(packed, "label", axis=0, tiled=True)
-    all_cent = lax.all_gather(centroids, "doc", axis=0, tiled=True)
-    gathered, all_cent = lax.optimization_barrier((gathered, all_cent))
-    rows = gathered[:, :width]
-    ints_rows = gathered[:, width : width + short + 2 * n_pos].astype(jnp.int32)
+    all_cent = lax.all_to_all(
+        jnp.broadcast_to(centroids[None], (n_doc,) + centroids.shape).reshape(n_doc * per_doc, width),
+        "doc", 0, 0, tiled=True,
+    )
+    n_clusters = all_cent.shape[0]
     short_rows = ints_rows[:, :short]
     pcl_rows = ints_rows[:, short : short + n_pos]
-    pos_rows = pcl_rows * CLS + ints_rows[:, short + n_pos :]
+    pos_local = pcl_rows * CLS + ints_rows[:, short + n_pos :] - cluster_base * CLS
+    local_clusters = cluster_base + jnp.arange(cl_here, dtype=jnp.int32)
+    member = jnp.any(short_rows[:, :, None] == local_clusters[None, None, :], axis=1)
+    member = member.astype(jnp.float32)
 
-    n_clusters = all_cent.shape[0]
+    rows = lax.all_gather(doc_embed, "label", axis=0, tiled=True)
+    rows, all_cent, member, pos_local, pcl_rows = lax.optimization_barrier(
+        (rows, all_cent, member, pos_local, pcl_rows)
+    )
 
-    local_clusters = cluster_base + jnp.arange(cl_here, dtype=jnp.int32)
     logits = jnp.einsum("nd,ld->nl", rows, classifier, preferred_element_type=jnp.float32)
-    member = jnp.any(short_rows[:, :, None] == local_clusters[None, None, :], axis=1)
-    pos_local = pos_rows - cluster_base * CLS
     label_ids = jnp.arange(labels_dev, dtype=jnp.int32).reshape(1, cl_here, CLS)
     target = pos_local[:, 0, None, None] == label_ids
     for p in range(1, n_pos):
@@ -46,7 +50,7 @@
     grad = (
         LOSS_WEIGHT
         * (jax.nn.sigmoid(logits.reshape(-1, cl_here, CLS)) - target.astype(jnp.float32))
-        * member[:, :, None].astype(jnp.float32)
+        * member[:, :, None]
     ).astype(jnp.bfloat16).reshape(-1, labels_dev)
 
     docs_part = jnp.dot(grad, classifier, preferred_element_type=jnp.float32).astype(jnp.bfloat16)

time: 265 us -> 259 us (0.977)
  blocking collectives: 91.4 us -> 53.9 us
  starting transfers between devices: 4.83 us -> 25.8 us
  waiting for transfers between devices: 124 us -> 135 us
    all_gather x1 -> x0, blocking collectives: 37.5 us -> none  [step(): all_cent = lax.all_gather(centroids, 'doc', axis=0, tiled=True)]
    all_to_all x0 -> x2, starting transfers between devices: none -> 21 us  [the longest x1 13.2 us: step(): lax.all_to_all(jnp.broadcast_to(ints[None], (n_label,) + ints.shape).resh...]
    all_to_all x0 -> x2, waiting for transfers between devices: none -> 20.5 us  [the longest x1 11.9 us: step(): lax.all_to_all(jnp.broadcast_to(ints[None], (n_label,) + ints.shape).resh...]
    all_gather x1, waiting for transfers between devices: 26.7 us -> 15.8 us  [step(): rows = lax.all_gather(doc_embed, 'label', axis=0, tiled=True)]
  transfers between devices with their start and end apart: 3 -> 5, of which waited for: 2 -> 4; matrix products, arithmetic and copies ran while one was open for 3% -> 6% of each run, Pallas kernels for 0% -> 0%
where the time goes in v3:
time: 259 us; the launch traced here: 258 us
  waiting for transfers between devices  135 us (52%)
  blocking collectives  53.9 us (21%)
  starting transfers between devices  25.8 us (10%)
  between operations  14.3 us (6%)
  matrix products  13.6 us (5%)
  local copies, waits for them, and re-layouts  11.4 us (4%)
  other arithmetic  4.73 us (2%)
    reduce_scatter x1, waiting for transfers between devices, step(): lax.psum_scatter(docs_part, 'label', scatter_dimension=0, tiled=True)  97.6 us
    all_to_all x1, blocking collectives, step(): recv = lax.all_to_all(send, 'doc', 0, 0, tiled=True)  53.9 us
    all_gather x1, waiting for transfers between devices, step(): rows = lax.all_gather(doc_embed, 'label', axis=0, tiled=True)  15.8 us
    all_to_all x1, starting transfers between devices, step(): lax.all_to_all(jnp.broadcast_to(ints[None], (n_label,) + ints.shape).resh...  13.2 us
    all_to_all x1, waiting for transfers between devices, step(): lax.all_to_all(jnp.broadcast_to(ints[None], (n_label,) + ints.shape).resh...  11.9 us
    all_to_all x1, waiting for transfers between devices, step(): lax.all_to_all(jnp.broadcast_to(centroids[None], (n_doc,) + centroids.sha...  8.59 us
    all_to_all x1, starting transfers between devices, step(): lax.all_to_all(jnp.broadcast_to(centroids[None], (n_doc,) + centroids.sha...  7.82 us
  transfers between devices with their start and end apart: 5, of which 4 were waited for; matrix products, arithmetic and copies ran while one was open for 6% of the time, Pallas kernels for 0%

profile of v3, /device:TPU:8, one launch (start us, length us, event | category | flops | bytes accessed | tf_op | source)
XLA Modules:
  0.0 258.3 jit_solution(17132346932606121884)
XLA Ops:
  7.2 0.7 all-gather.2.cloned.1.call-update
  7.9 0.7 bitcast_or_fusion
  8.9 1.3 gather_fusion
  10.7 1.1 reshape.124
  11.8 13.2 %all-to-all-start.1 = ((s32[32,1,1280]{2,1,0:T(1,128)}), s32[32,1,1280]{2,1,0:T(1,128)S(1)}, u32[]{:S(2)}, u32[]{:S(2)}) async-start(s32[32,1,1280]{2,1,0:T(1,128)} %reshape.124), calls=%async_computation.1 | async-start | bytes 327680 | tf_op jit(solution)/shard_map/all_to_all | solution.py:24
  24.9 11.9 %all-to-all-done.1 = s32[32,1,1280]{2,1,0:T(1,128)S(1)} async-done(((s32[32,1,1280]{2,1,0:T(1,128)}), s32[32,1,1280]{2,1,0:T(1,128)S(1)}, u32[]{:S(2)}, u32[]{:S(2)}) %all-to-all-start.1) | async-done | bytes 163872 | tf_op jit(solution)/shard_map/all_to_all | solution.py:24
  36.8 0.8 broadcast_in_dim.10
  37.6 7.8 %all-to-all-start = ((bf16[16,16,768]{2,1,0:T(8,128)(2,1)}), bf16[16,16,768]{2,1,0:T(8,128)(2,1)S(1)}, u32[]{:S(2)}, u32[]{:S(2)}) async-start(bf16[16,16,768]{2,1,0:T(8,128)(2,1)} %broadcast_in_dim.10), calls=%async_computation | async-start | bytes 786432 | tf_op jit(solution)/shard_map/all_to_all | solution.py:28
  47.0 1.0 reduce.1
  49.4 0.8 compare_reduce_fusion
  50.2 8.6 %all-to-all-done = bf16[16,16,768]{2,1,0:T(8,128)(2,1)S(1)} async-done(((bf16[16,16,768]{2,1,0:T(8,128)(2,1)}), bf16[16,16,768]{2,1,0:T(8,128)(2,1)S(1)}, u32[]{:S(2)}, u32[]{:S(2)}) %all-to-all-start) | async-done | bytes 393248 | tf_op jit(solution)/shard_map/all_to_all | solution.py:28
  58.8 15.8 %all-gather.2.cloned.1.call-done = bf16[1024,768]{1,0:T(8,128)(2,1)} async-done(((bf16[32,768]{1,0:T(8,128)(2,1)}), bf16[1024,768]{1,0:T(8,128)(2,1)}) %all-gather.2.cloned.1.call-update) | async-done | bytes 1572880 | tf_op jit(solution)/shard_map/all_gather | solution.py:40
  74.9 1.1 mul.44
  76.3 3.6 %fusion = bf16[1024,1024]{1,0:T(8,128)(2,1)S(1)} fusion(f32[128,8,8,128]{3,2,1,0:T(8,128)S(1)} %bitcast.38, bf16[1024,768]{1,0:T(8,128)(2,1)S(1)} %copy-done.2, bf16[1024,768]{1,0:T(8,128)(2,1)S(1)} %copy-done, s32[1024]{0:T(1024)S(1)} %copy-done.7, s32[1024]{0:T(1024)S(1)} %bitcast.44, s32[1024]{0:T(1024)S(1)} %bitcast.45, s32[1024]{0:T(1024)S(1)} %bitcast.46, ...), kind=kOutput, calls=%fused_computation.2 | convolution fusion | flops 1625292800 | bytes 9457664 | tf_op jit(solution)/shard_map/nd,ld->nl/dot_general | solution.py:45
  79.9 1.9 convolution_convert_fusion.1
  81.8 1.2 fusion.6
  83.9 53.9 %all_to_all.33 = bf16[16,80,768]{2,1,0:T(8,128)(2,1)S(1)} all-to-all(bf16[16,80,768]{2,1,0:T(8,128)(2,1)S(1)} %pad_maximum_fusion), channel_id=1, replica_groups=mesh['doc'=16,'label'=32] {'doc'}, dimensions={0} | all-to-all | bytes 3932160 | tf_op jit(solution)/shard_map/all_to_all | solution.py:79
  138.0 1.3 broadcast_in_dim.13
  139.3 4.8 %all-to-all-start.3 = ((bf16[16,64,768]{2,1,0:T(8,128)(2,1)}), bf16[16,64,768]{2,1,0:T(8,128)(2,1)}, u32[]{:S(2)}, u32[]{:S(2)}) async-start(bf16[16,64,768]{2,1,0:T(8,128)(2,1)} %broadcast_in_dim.13), calls=%async_computation.3 | async-start | bytes 3145728 | tf_op jit(solution)/shard_map/all_to_all | solution.py:84
  144.1 4.5 %convolution_convert_fusion = bf16[1024,768]{1,0:T(8,128)(2,1)} fusion(bf16[1024,1024]{1,0:T(8,128)(2,1)} %copy-done.8, bf16[1024,768]{1,0:T(8,128)(2,1)S(1)} %copy-done), kind=kOutput, calls=%fused_computation.4 | convolution fusion | flops 1611399168 | bytes 5242880 | tf_op jit(solution)/shard_map/dot_general | solution.py:56
  148.7 97.6 %reduce-scatter.2.cloned.1.call-done = bf16[32,768]{1,0:T(8,128)(2,1)} async-done(((bf16[1024,768]{1,0:T(8,128)(2,1)}), bf16[32,768]{1,0:T(8,128)(2,1)}) %reduce-scatter.2.cloned.1.call-update) | async-done | bytes 49168 | tf_op jit(solution)/shard_map/reduce_scatter | solution.py:57
  246.3 1.8 fusion.7
  248.1 0.7 convert_reduce_fusion
  248.8 2.7 %copy.59 = bf16[1024,768]{1,0:T(8,128)(2,1)} copy(bf16[1024,768]{1,0:T(8,128)(2,1)} %bitcast.14) | data formatting | bytes 3145728
  (48 shorter events, 5.4 us)
Async XLA Ops:
  7.2 68.9 %copy-start = (bf16[1024,768]{1,0:T(8,128)(2,1)S(1)}, bf16[1024,768]{1,0:T(8,128)(2,1)}, u32[]{:S(2)}) copy-start(bf16[1024,768]{1,0:T(8,128)(2,1)} %param.6) | copy-start | bytes 4718596
  7.2 1.6 copy-start.1
  7.2 67.4 %all-gather.2.cloned.1.call-start = ((), (), s32[]{:S(2)}) async-start(), calls=%async_computation.5 | async-start | bytes 1622016 | tf_op jit(solution)/shard_map/all_gather | solution.py:40
  8.8 1.5 copy-start.6
  8.8 28.0 %copy-start.5 = (bf16[16,768]{1,0:T(8,128)(2,1)S(1)}, bf16[16,768]{1,0:T(8,128)(2,1)}, u32[]{:S(2)}) copy-start(bf16[16,768]{1,0:T(8,128)(2,1)} %param.7) | copy-start | bytes 73732
  11.8 25.0 %all-to-all-start.1 = ((s32[32,1,1280]{2,1,0:T(1,128)}), s32[32,1,1280]{2,1,0:T(1,128)S(1)}, u32[]{:S(2)}, u32[]{:S(2)}) async-start(s32[32,1,1280]{2,1,0:T(1,128)} %reshape.124), calls=%async_computation.1 | async-start | bytes 327680 | tf_op jit(solution)/shard_map/all_to_all | solution.py:24
  37.6 21.2 %all-to-all-start = ((bf16[16,16,768]{2,1,0:T(8,128)(2,1)}), bf16[16,16,768]{2,1,0:T(8,128)(2,1)S(1)}, u32[]{:S(2)}, u32[]{:S(2)}) async-start(bf16[16,16,768]{2,1,0:T(8,128)(2,1)} %broadcast_in_dim.10), calls=%async_computation | async-start | bytes 786432 | tf_op jit(solution)/shard_map/all_to_all | solution.py:28
  58.8 23.0 %copy-start.3 = (bf16[16,16,768]{2,1,0:T(8,128)(2,1)}, bf16[16,16,768]{2,1,0:T(8,128)(2,1)S(1)}, u32[]{:S(2)}) copy-start(bf16[16,16,768]{2,1,0:T(8,128)(2,1)S(1)} %all-to-all-done) | copy-start | bytes 1179652
  74.9 1.4 copy-start.2
  74.9 1.4 copy-start.7
  79.9 1.9 copy-start.8
  83.0 0.8 copy-start.4
  139.3 109.4 %all-to-all-start.3 = ((bf16[16,64,768]{2,1,0:T(8,128)(2,1)}), bf16[16,64,768]{2,1,0:T(8,128)(2,1)}, u32[]{:S(2)}, u32[]{:S(2)}) async-start(bf16[16,64,768]{2,1,0:T(8,128)(2,1)} %broadcast_in_dim.13), calls=%async_computation.3 | async-start | bytes 3145728 | tf_op jit(solution)/shard_map/all_to_all | solution.py:84
  144.1 102.2 %reduce-scatter.2.cloned.1.call-start = ((), (), s32[]{:S(2)}) async-start(), calls=%async_computation.6 | async-start | bytes 1622016 | tf_op jit(solution)/shard_map/reduce_scatter | solution.py:57
Sparse Core Ops, SparseCore 0:
  11.1 63.4 all-gather.1
  149.3 96.9 reduce-scatter.1
